TPU v7x, 128 devices: a whole 4x4x4 slice. The times are simulated.
128 devices in a mesh: tok: 16 (over y, x), head: 8 (over z, core).
Axes of the slice: x: 4, y: 4, z: 4, core: 2. Of those that a mesh axis runs over, the one named last changes fastest.
Arguments:
- tokens: bfloat16 [8192, 8192], P('tok', 'head'), may hold values from -60 to 60
- gain: bfloat16 [8192], P('head'), may hold values from 0.5 to 2
- w_query: bfloat16 [8192, 8, 512], P(('head', 'tok')), may hold values from -0.125 to 0.125
- w_key: bfloat16 [8192, 8, 128], P(('head', 'tok')), may hold values from -0.0625 to 0.0625
- w_value: bfloat16 [8192, 8, 128], P(('head', 'tok')), may hold values from -0.5 to 0.5
- group_ids: int32 [8192, 1], P('tok'), may hold values from 0 to 15; in each aligned block of 512 rows (0 to 511, 512 to 1023, ...) at most 64 rows name the same one
- key_pages: bfloat16 [1024, 128, 8, 128], P('tok', None, 'head'), may hold values from -42 to 42
- value_pages: bfloat16 [1024, 128, 8, 128], P('tok', None, 'head'), may hold values from -48 to 48
- page_table: int32 [16, 32], P('tok'), may hold values from 0 to 1023, as said below
Outputs:
- attention: bfloat16 [8192, 4096], P('tok', 'head')
Inputs may be any that keep to these rules, and one draw needn't show every extreme that they name: `group_ids`: among the 512 tokens of one index of tok (aligned blocks of rows), no group appears more than 64 times, a bound that some block reaches. `page_table`: row g lists 32 different pages, all in g * 64 to (g + 1) * 64 - 1, among them the first and the last page of that range.
All inputs are finite; a program needn't handle non-finite values.
Results may differ from a plain program's by a relative error of at most 0.0085.
The roundings to bfloat16 on the way count: a program that leaves them out, or rounds other values in their place, can miss the bound.
Values may be sent and summed in bfloat16 or wider, within the bound.
No kernel may reach another device: no remote copies, remote signals or barrier semaphores. Data moves between devices by JAX's collectives and lax.ppermute only.
A program may use at most 128 MiB of HBM per device.

v0:
```python
import math
import jax
import jax.numpy as jnp
from jax import lax
from jax.sharding import PartitionSpec as P

EPS = 1e-05
THETA = 10000.0


def rotate(values, positions):
    halfway = values.shape[-1] // 2
    frequency = jnp.exp(
        -math.log(THETA) * 2.0 * jnp.arange(halfway, dtype=jnp.float32) / values.shape[-1]
    )
    angles = positions.astype(jnp.float32)[:, None] * frequency[None, :]
    cosine = jnp.cos(angles)[:, None, :]
    sine_part = jnp.sin(angles)[:, None, :]
    leading = values[..., :halfway].astype(jnp.float32)
    trailing = values[..., halfway:].astype(jnp.float32)
    return jnp.concatenate(
        [leading * cosine - trailing * sine_part, trailing * cosine + leading * sine_part], axis=-1
    ).astype(jnp.bfloat16)


def attend(
    queries, query_rank, prefix_keys, prefix_values, new_keys, new_values, key_rank, key_live
):
    scaling = 1.0 / math.sqrt(queries.shape[-1])
    before = (
        jnp.einsum("bhd,pd->bhp", queries, prefix_keys, preferred_element_type=jnp.float32)
        * scaling
    )
    inside = (
        jnp.einsum("bhd,sd->bhs", queries, new_keys, preferred_element_type=jnp.float32) * scaling
    )
    allowed = key_live[None, :] & (key_rank[None, :] <= query_rank[:, None])
    inside = jnp.where(allowed[:, None, :], inside, -jnp.inf)
    highest = jnp.maximum(jnp.max(before, axis=-1), jnp.max(inside, axis=-1))
    expo_before = jnp.exp(before - highest[..., None])
    expo_inside = jnp.exp(inside - highest[..., None])
    totals = jnp.sum(expo_before, axis=-1) + jnp.sum(expo_inside, axis=-1)
    mixed = jnp.einsum(
        "bhp,pd->bhd",
        expo_before.astype(jnp.bfloat16),
        prefix_values,
        preferred_element_type=jnp.float32,
    )
    mixed = mixed + jnp.einsum(
        "bhs,sd->bhd",
        expo_inside.astype(jnp.bfloat16),
        new_values,
        preferred_element_type=jnp.float32,
    )
    return (mixed / totals[..., None]).astype(jnp.bfloat16)


def row_norm(tokens, gain, full_width):
    values_wide = tokens.astype(jnp.float32)
    squares = lax.psum(jnp.sum(values_wide * values_wide, axis=1), "head")
    factor = lax.rsqrt(squares / full_width + EPS)
    return (values_wide * factor[:, None] * gain.astype(jnp.float32)[None, :]).astype(jnp.bfloat16)


def body(tokens, gain, w_query, w_key, w_value, group_ids, key_pages, value_pages, page_table):
    row_count = tokens.shape[0]
    n_tok = lax.axis_size("tok")
    n_head = lax.axis_size("head")
    head_size = key_pages.shape[-1]
    query_width = w_query.shape[2]
    group_heads = query_width // head_size
    full_width = tokens.shape[1] * n_head
    capacity = 2 * row_count // n_tok
    normed = row_norm(tokens, gain, full_width)
    weights_local = jnp.concatenate([w_query, w_key, w_value], axis=2)
    gathered = lax.all_gather(weights_local, "tok", axis=0, tiled=True)
    group_count = row_count * lax.axis_size("head") // row_count
    joined = jnp.einsum("rd,dnc->nrc", normed, gathered, preferred_element_type=jnp.float32)
    projected = lax.psum_scatter(
        joined.reshape(group_count * row_count, joined.shape[2]),
        "head",
        scatter_dimension=0,
        tiled=True,
    )
    projected_low = projected.astype(jnp.bfloat16)
    width_all = projected_low.shape[1]
    group_of = group_ids[:, 0]
    member = (group_of[:, None] == jnp.arange(n_tok, dtype=jnp.int32)[None, :]).astype(jnp.int32)
    local_rank = jnp.sum((jnp.cumsum(member, axis=0) - member) * member, axis=1)
    slot_index = group_of * capacity + local_rank
    outgoing = (
        jnp.zeros((n_tok * capacity, width_all), jnp.bfloat16).at[slot_index].set(projected_low)
    )
    arrived = lax.all_to_all(
        outgoing.reshape(n_tok, capacity, width_all), "tok", split_axis=0, concat_axis=0, tiled=True
    )
    all_groups = lax.all_gather(group_of, "tok", axis=0, tiled=True).reshape(n_tok, row_count)
    block_counts = jnp.sum((all_groups == lax.axis_index("tok")).astype(jnp.int32), axis=1)
    slot_total = n_tok * capacity
    arrived = arrived.reshape(slot_total, width_all)
    live_count = (
        (jnp.arange(capacity, dtype=jnp.int32)[None, :] < block_counts[:, None])
        .astype(jnp.int32)
        .reshape(slot_total)
    )
    key_live = live_count > 0
    slot_rank = jnp.cumsum(live_count) - live_count
    prefix_length = page_table.shape[1] * key_pages.shape[1]
    positions = prefix_length + slot_rank
    rotated_queries = rotate(
        arrived[:, :query_width].reshape(slot_total, group_heads, head_size), positions
    )
    rotated_keys = rotate(
        arrived[:, query_width : query_width + head_size].reshape(slot_total, 1, head_size),
        positions,
    )[:, 0, :]
    slot_values = arrived[:, query_width + head_size :]
    local_pages = page_table[0] - lax.axis_index("tok") * key_pages.shape[0]
    prefix_keys = jnp.take(key_pages[:, :, 0, :], local_pages, axis=0).reshape(
        prefix_length, head_size
    )
    prefix_values = jnp.take(value_pages[:, :, 0, :], local_pages, axis=0).reshape(
        prefix_length, head_size
    )
    block_size = min(128, slot_total)

    def one_block(blocked):
        return attend(
            blocked[0],
            blocked[1],
            prefix_keys,
            prefix_values,
            rotated_keys,
            slot_values,
            slot_rank,
            key_live,
        )

    attended = lax.map(
        one_block,
        (
            rotated_queries.reshape(slot_total // block_size, block_size, group_heads, head_size),
            slot_rank.reshape(slot_total // block_size, block_size),
        ),
    )
    returned = lax.all_to_all(
        attended.reshape(n_tok, capacity, query_width),
        "tok",
        split_axis=0,
        concat_axis=0,
        tiled=True,
    )
    return returned.reshape(n_tok * capacity, query_width)[slot_index]


def solution(mesh):
    placed = (
        P("tok", "head"),
        P("head"),
        P(("head", "tok"), None, None),
        P(("head", "tok"), None, None),
        P(("head", "tok"), None, None),
        P("tok", None),
        P("tok", None, "head", None),
        P("tok", None, "head", None),
        P("tok", None),
    )
    return jax.shard_map(
        body, mesh=mesh, in_specs=placed, out_specs=P("tok", "head"), check_vma=False
    )
```

profile of v0, /device:TPU:32, one launch (start us, length us, event | category | flops | bytes accessed | tf_op | source)
XLA Modules:
  0.0 349.9 jit_solution(17621018906772747158)
XLA Ops:
  11.1 12.5 %psum.7 = f32[512]{0:T(512)S(1)} all-reduce(f32[512]{0:T(512)S(1)} %fusion.33), channel_id=1, replica_groups=mesh['tok'=16,'head'=8] {'head'}, use_global_device_ids=true, to_apply=%region_4.5 | all-reduce | flops 512 | bytes 4096 | tf_op jit(solution)/shard_map/psum | solution.py:60
  23.6 78.9 %all-gather.3.cloned.1.call-done = bf16[1024,8,768]{2,0,1:T(8,128)(2,1)} async-done(((bf16[64,8,768]{2,0,1:T(8,128)(2,1)}), bf16[1024,8,768]{2,0,1:T(8,128)(2,1)}) %all-gather.3.cloned.1.call-update) | async-done | bytes 12582928 | tf_op jit(solution)/shard_map/all_gather | solution.py:76
  102.5 14.4 %fusion.41 = f32[8,768,512]{1,2,0:T(8,128)} fusion(bf16[1024,8,768]{2,0,1:T(8,128)(2,1)} %all-gather.3.cloned.1.call-done, bf16[512,1024]{1,0:T(8,128)(2,1)S(1)} %copy-done.2, f32[1024]{0:T(1024)S(1)} %convert_element_type.78, f32[512]{0:T(512)S(1)} %add_rsqrt_fusion), kind=kOutput, calls=%fused_computation.58 | convolution fusion | flops 6444548096 | bytes 26220544 | tf_op jit(solution)/shard_map/rd,dnc->nrc/dot_general | solution.py:78
  117.6 23.0 %all-gather = s32[8192,1]{0,1:T(1,128)S(1)} all-gather(s32[512,1]{0,1:T(1,128)S(1)} %copy-done.4), channel_id=2, replica_groups=mesh['tok'=16,'head'=8] {'tok'}, dimensions={0}, use_global_device_ids=true | all-gather | bytes 34816 | tf_op jit(solution)/shard_map/all_gather | solution.py:97
  143.2 43.5 %reduce-scatter.2.cloned.1.call-done = f32[512,768]{1,0:T(8,128)} async-done(((f32[4096,768]{1,0:T(8,128)}), f32[512,768]{1,0:T(8,128)}) %reduce-scatter.2.cloned.1.call-update) | async-done | bytes 1572880 | tf_op jit(solution)/shard_map/reduce_scatter | solution.py:79
  186.7 4.6 %scatter_custom_fusion = bf16[1024,768]{1,0:T(8,128)(2,1)} fusion(s32[512]{0:T(512)S(1)} %bitcast.121, f32[512,768]{1,0:T(8,128)} %reduce-scatter.2.cloned.1.call-done, bf16[]{:T(256)} %constant.32.clone.1), kind=kCustom, calls=%fused_computation.65 | custom fusion | flops 393216 | bytes 3145730 | tf_op jit(solution)/shard_map/scatter | solution.py:92
  191.4 7.2 %all-to-all-start = ((bf16[16,64,768]{2,1,0:T(8,128)(2,1)}), bf16[16,64,768]{2,1,0:T(8,128)(2,1)}, u32[]{:S(2)}, u32[]{:S(2)}) async-start(bf16[16,64,768]{2,1,0:T(8,128)(2,1)} %bitcast.112), calls=%async_computation.1 | async-start | bytes 3145728 | tf_op jit(solution)/shard_map/all_to_all | solution.py:94
  198.7 1.7 gather_fusion.1
  200.3 3.2 gather_fusion.2
  203.8 1.7 multiply_cosine_fusion.1
  205.6 2.8 broadcast_select_fusion
  208.4 18.2 %all-to-all-done = bf16[16,64,768]{2,1,0:T(8,128)(2,1)} async-done(((bf16[16,64,768]{2,1,0:T(8,128)(2,1)}), bf16[16,64,768]{2,1,0:T(8,128)(2,1)}, u32[]{:S(2)}, u32[]{:S(2)}) %all-to-all-start) | async-done | bytes 1572896 | tf_op jit(solution)/shard_map/all_to_all | solution.py:94
  226.6 1.8 fusion.64
  228.4 2.3 slice.52
  230.6 3.1 fusion.57
  233.7 2.3 copy.21
  236.0 1.6 fusion.37
  239.0 2.4 copy.19
  242.6 73.7 %while.11 = (s32[]{:T(128)}, bf16[8,128,4,128]{3,2,1,0:T(4,128)(2,1)}, bf16[8,128,4,128]{3,1,2,0:T(8,128)(2,1)}, bf16[4096,128]{1,0:T(8,128)(2,1)}, s32[1024]{0:...) while((s32[]{:T(128)}, ...), condition=%wide.region_15.17_spmd.clone, body=%wide.region_10.16_spmd.clone.sunk | while | flops 1365182464 | bytes 41082088 | solution.py:139
  244.5 2.3 multiply_reduce_fusion.2
  253.7 2.3 multiply_reduce_fusion.2
  262.9 2.3 multiply_reduce_fusion.2
  272.1 2.3 multiply_reduce_fusion.2
  279.8 1.6 fusion.83
  281.3 2.3 multiply_reduce_fusion.2
  290.5 2.3 multiply_reduce_fusion.2
  299.8 2.3 multiply_reduce_fusion.2
  309.0 2.3 multiply_reduce_fusion.2
  316.3 2.3 reshape.284
  318.6 3.7 %all-to-all-start.1 = ((bf16[16,64,512]{2,1,0:T(8,128)(2,1)}), bf16[16,64,512]{2,1,0:T(8,128)(2,1)S(1)}, u32[]{:S(2)}, u32[]{:S(2)}) async-start(bf16[16,64,512]{2,1,0:T(8,128)(2,1)} %reshape.284), calls=%async_computation.2 | async-start | bytes 2097152 | tf_op jit(solution)/shard_map/all_to_all | solution.py:146
  322.2 18.2 %all-to-all-done.1 = bf16[16,64,512]{2,1,0:T(8,128)(2,1)S(1)} async-done(((bf16[16,64,512]{2,1,0:T(8,128)(2,1)}), bf16[16,64,512]{2,1,0:T(8,128)(2,1)S(1)}, u32[]{:S(2)}, u32[]{:S(2)}) %all-to-all-start.1) | async-done | bytes 1048608 | tf_op jit(solution)/shard_map/all_to_all | solution.py:146
  340.5 2.6 gather_fusion
  (189 shorter events, 64.3 us)
Async XLA Ops:
  6.5 192.1 %copy-start = (bf16[64,128,1,128]{3,1,2,0:T(8,128)(2,1)S(1)}, bf16[64,128,1,128]{3,1,2,0:T(8,128)(2,1)}, u32[]{:S(2)}) copy-start(bf16[64,128,1,128]{3,1,2,0:T(8,128)(2,1)} %param.19) | copy-start | bytes 6291460
  6.5 4.2 %copy-start.5 = (bf16[1024]{0:T(1024)(128)(2,1)S(1)}, bf16[1024]{0:T(1024)(128)(2,1)}, u32[]{:S(2)}) copy-start(bf16[1024]{0:T(1024)(128)(2,1)} %param.14) | copy-start | bytes 6148
  6.5 4.3 %copy-start.2 = (bf16[512,1024]{1,0:T(8,128)(2,1)S(1)}, bf16[512,1024]{1,0:T(8,128)(2,1)}, u32[]{:S(2)}) copy-start(bf16[512,1024]{1,0:T(8,128)(2,1)} %param.13) | copy-start | bytes 3145732
  6.5 96.0 %all-gather.3.cloned.1.call-start = ((), (), s32[]{:S(2)}) async-start(), calls=%async_computation.3 | async-start | bytes 13369344 | tf_op jit(solution)/shard_map/all_gather | solution.py:76
  10.7 176.0 %reduce-scatter.2.cloned.1.call-start = ((), (), s32[]{:S(2)}) async-start(), calls=%async_computation.4 | async-start | bytes 14155776 | tf_op jit(solution)/shard_map/reduce_scatter | solution.py:79
  116.9 0.7 copy-start.4
  191.4 7.2 %copy-start.6 = (s32[1,32]{1,0:T(1,128)S(1)}, s32[1,32]{1,0:T(1,128)}, u32[]{:S(2)}) copy-start(s32[1,32]{1,0:T(1,128)} %param.21) | copy-start | bytes 388
  191.4 35.2 %all-to-all-start = ((bf16[16,64,768]{2,1,0:T(8,128)(2,1)}), bf16[16,64,768]{2,1,0:T(8,128)(2,1)}, u32[]{:S(2)}, u32[]{:S(2)}) async-start(bf16[16,64,768]{2,1,0:T(8,128)(2,1)} %bitcast.112), calls=%async_computation.1 | async-start | bytes 3145728 | tf_op jit(solution)/shard_map/all_to_all | solution.py:94
  242.8 1.7 copy-start.1
  248.9 1.5 copy-start.3
  252.0 1.7 copy-start.1
  258.1 1.5 copy-start.3
  261.2 1.7 copy-start.1
  267.3 1.5 copy-start.3
  270.4 1.7 copy-start.1
  276.5 1.5 copy-start.3
  279.6 1.7 copy-start.1
  285.7 1.5 copy-start.3
  288.8 1.7 copy-start.1
  294.9 1.5 copy-start.3
  298.0 1.7 copy-start.1
  304.1 1.5 copy-start.3
  307.2 1.7 copy-start.1
  313.3 1.5 copy-start.3
  318.6 21.9 %all-to-all-start.1 = ((bf16[16,64,512]{2,1,0:T(8,128)(2,1)}), bf16[16,64,512]{2,1,0:T(8,128)(2,1)S(1)}, u32[]{:S(2)}, u32[]{:S(2)}) async-start(bf16[16,64,512]{2,1,0:T(8,128)(2,1)} %reshape.284), calls=%async_computation.2 | async-start | bytes 2097152 | tf_op jit(solution)/shard_map/all_to_all | solution.py:146
Sparse Core Ops, SparseCore 0:
  10.9 91.6 all-gather.2
  117.1 69.6 reduce-scatter.1
where the time goes:
time: 351 us; the launch traced here: 350 us
  waiting for transfers between devices  159 us (45%)
  matrix products  62.2 us (18%)
  other arithmetic  38.3 us (11%)
  blocking collectives  35.5 us (10%)
  local copies, waits for them, and re-layouts  30.1 us (9%)
  between operations  13.6 us (4%)
  starting transfers between devices  10.9 us (3%)
    all_gather x1, waiting for transfers between devices, body(): gathered = lax.all_gather(weights_local, 'tok', axis=0, tiled=True)  78.9 us
    reduce_scatter x1, waiting for transfers between devices, body(): lax.psum_scatter(joined.reshape(group_count * row_count, joined.shape[2])...  43.5 us
    all_gather x1, blocking collectives, body(): lax.all_gather(group_of, 'tok', axis=0, tiled=True)  23 us
    all_to_all x1, waiting for transfers between devices, body(): lax.all_to_all(attended.reshape(n_tok, capacity, query_width), 'tok', spl...  18.2 us
    all_to_all x1, waiting for transfers between devices, body(): lax.all_to_all(outgoing.reshape(n_tok, capacity, width_all), 'tok', split...  18.2 us
    dot_general x8, matrix products, attend(): jnp.einsum('bhd,pd->bhp', queries, prefix_keys, preferred_element_type=jn...  18 us
    reduce_sum x16, other arithmetic, attend(): totals = jnp.sum(expo_before, axis=-1) + jnp.sum(expo_inside, axis=-1)  16.8 us
    dot_general x1, matrix products, body(): jnp.einsum('rd,dnc->nrc', normed, gathered, preferred_element_type=jnp.fl...  14.4 us
  transfers between devices with their start and end apart: 4, of which 4 were waited for; matrix products, arithmetic and copies ran while one was open for 4% of the time, Pallas kernels for 0%

commit v1 on v0

--- a/solution.py
+++ b/solution.py
@@ -6,6 +6,28 @@
 
 EPS = 1e-05
 THETA = 10000.0
+
+
+def in_order(pieces, dim):
+    lengths = list(pieces.shape[1:])
+    lengths[dim] *= pieces.shape[0]
+    return jnp.moveaxis(pieces, 0, dim).reshape(lengths)
+
+
+def gather_around(value, axis, dim):
+    devices = lax.axis_size(axis)
+    pairs = [(i, (i + 1) % devices) for i in range(devices)]
+    back = [(b, a) for a, b in pairs]
+    lower, upper = ([], [])
+    for step in range(devices - 1):
+        if step % 2 == 0:
+            lower.append(lax.ppermute(lower[-1] if lower else value, axis, pairs))
+        else:
+            upper.append(lax.ppermute(upper[-1] if upper else value, axis, back))
+    blocks = jnp.stack([*lower[::-1], value, *upper])
+    shift = lax.axis_index(axis) - len(lower)
+    blocks = blocks[(jnp.arange(devices) - shift) % devices]
+    return in_order(blocks, dim)
 
 
 def rotate(values, positions):
@@ -94,7 +116,7 @@
     arrived = lax.all_to_all(
         outgoing.reshape(n_tok, capacity, width_all), "tok", split_axis=0, concat_axis=0, tiled=True
     )
-    all_groups = lax.all_gather(group_of, "tok", axis=0, tiled=True).reshape(n_tok, row_count)
+    all_groups = gather_around(group_of, "tok", 0).reshape(n_tok, row_count)
     block_counts = jnp.sum((all_groups == lax.axis_index("tok")).astype(jnp.int32), axis=1)
     slot_total = n_tok * capacity
     arrived = arrived.reshape(slot_total, width_all)

time: 351 us -> 352 us (level)
  starting transfers between devices: 10.9 us -> 52.2 us
  blocking collectives: 35.5 us -> 12.5 us
  waiting for transfers between devices: 159 us -> 141 us
    ppermute x0 -> x15, starting transfers between devices: none -> 38.4 us  [the longest x7 36.9 us: gather_around(): upper.append(lax.ppermute(upper[-1] if upper else value, axis, back))]
    ppermute x0 -> x15, waiting for transfers between devices: none -> 24.4 us  [the longest x7 22.7 us: gather_around(): upper.append(lax.ppermute(upper[-1] if upper else value, axis, back))]
    all_gather x1 -> x0, blocking collectives: 23 us -> none  [body(): lax.all_gather(group_of, 'tok', axis=0, tiled=True)]
    reduce_scatter x1, waiting for transfers between devices: 43.5 us -> 20.9 us  [body(): lax.psum_scatter(joined.reshape(group_count * row_count, joined.shape[2])...]
    all_to_all x1, waiting for transfers between devices: 18.2 us -> 0.01 us  [body(): lax.all_to_all(outgoing.reshape(n_tok, capacity, width_all), 'tok', split...]
  transfers between devices with their start and end apart: 4 -> 19, of which waited for: 4 -> 13; matrix products, arithmetic and copies ran while one was open for 4% -> 6% of each run, Pallas kernels for 0% -> 0%
where the time goes in v1:
time: 352 us; the launch traced here: 351 us
  waiting for transfers between devices  141 us (40%)
  matrix products  60.7 us (17%)
  starting transfers between devices  52.2 us (15%)
  other arithmetic  39.5 us (11%)
  local copies, waits for them, and re-layouts  31.4 us (9%)
  between operations  13.6 us (4%)
  blocking collectives  12.5 us (4%)
    all_gather x1, waiting for transfers between devices, body(): gathered = lax.all_gather(weights_local, 'tok', axis=0, tiled=True)  77.7 us
    ppermute x7, starting transfers between devices, gather_around(): upper.append(lax.ppermute(upper[-1] if upper else value, axis, back))  36.9 us
    ppermute x7, waiting for transfers between devices, gather_around(): upper.append(lax.ppermute(upper[-1] if upper else value, axis, back))  22.7 us
    reduce_scatter x1, waiting for transfers between devices, body(): lax.psum_scatter(joined.reshape(group_count * row_count, joined.shape[2])...  20.9 us
    dot_general x8, matrix products, attend(): jnp.einsum('bhd,pd->bhp', queries, prefix_keys, preferred_element_type=jn...  18 us
    all_to_all x1, waiting for transfers between devices, body(): lax.all_to_all(attended.reshape(n_tok, capacity, query_width), 'tok', spl...  17.8 us
    reduce_sum x16, other arithmetic, attend(): totals = jnp.sum(expo_before, axis=-1) + jnp.sum(expo_inside, axis=-1)  16.8 us
    dot_general x1, matrix products, body(): jnp.einsum('rd,dnc->nrc', normed, gathered, preferred_element_type=jnp.fl...  12.8 us
  transfers between devices with their start and end apart: 19, of which 13 were waited for; matrix products, arithmetic and copies ran while one was open for 6% of the time, Pallas kernels for 0%

profile of v1, /device:TPU:32, one launch (start us, length us, event | category | flops | bytes accessed | tf_op | source)
XLA Modules:
  0.0 351.0 jit_solution(12852378271746348801)
XLA Ops:
  12.3 12.5 %psum.7 = f32[512]{0:T(512)S(1)} all-reduce(f32[512]{0:T(512)S(1)} %fusion.33), channel_id=1, replica_groups=mesh['tok'=16,'head'=8] {'head'}, use_global_device_ids=true, to_apply=%region_4.5 | all-reduce | flops 512 | bytes 4096 | tf_op jit(solution)/shard_map/psum | solution.py:82
  24.8 77.7 %all-gather.2.cloned.1.call-done = bf16[1024,8,768]{2,0,1:T(8,128)(2,1)} async-done(((bf16[64,8,768]{2,0,1:T(8,128)(2,1)}), bf16[1024,8,768]{2,0,1:T(8,128)(2,1)}) %all-gather.2.cloned.1.call-update) | async-done | bytes 12582928 | tf_op jit(solution)/shard_map/all_gather | solution.py:98
  102.6 12.8 %fusion.41 = f32[8,768,512]{1,2,0:T(8,128)} fusion(bf16[1024,8,768]{2,0,1:T(8,128)(2,1)} %all-gather.2.cloned.1.call-done, bf16[512,1024]{1,0:T(8,128)(2,1)} %param.13, f32[1024]{0:T(1024)S(1)} %convert_element_type.75, f32[512]{0:T(512)S(1)} %add_rsqrt_fusion), kind=kOutput, calls=%fused_computation.59 | convolution fusion | flops 6444548096 | bytes 26220544 | tf_op jit(solution)/shard_map/rd,dnc->nrc/dot_general | solution.py:100
  117.6 3.9 %collective-permute-start.8 = (s32[512]{0:T(512)S(1)}, s32[512]{0:T(512)S(1)}, u32[]{:S(2)}, u32[]{:S(2)}) collective-permute-start(s32[512]{0:T(512)S(1)} %bitcast.138), channel_id=1, source_target_pairs={{8,0},{16,8},{24,16},{32,24},{40,32},{48,40},{56,48},{64,56},{72,6... | collective-permute-start | bytes 6152 | tf_op jit(solution)/shard_map/ppermute | solution.py:26
  123.1 3.9 %gather_fusion.3 = bf16[32,128,128]{2,1,0:T(8,128)(2,1)} fusion(bf16[64,128,128]{2,1,0:T(8,128)(2,1)} %bitcast.136, s32[1024]{0:T(1024)S(1)} %pad_clamp_fusion.1), kind=kCustom, calls=%fused_computation.1.clone | custom fusion | bytes 2097280 | tf_op jit(solution)/shard_map/jit(_take)/gather | solution.py:144
  127.0 2.8 broadcast_select_fusion
  131.0 5.4 %collective-permute-start.9 = (s32[512]{0:T(512)S(1)}, s32[512]{0:T(512)S(1)}, u32[]{:S(2)}, u32[]{:S(2)}) collective-permute-start(s32[512]{0:T(512)S(1)} %collective-permute-done.8), channel_id=1, source_target_pairs={{8,0},{16,8},{24,16},{32,24},{40,32},{48,40},{56,48},{64,56},{72,6... | collective-permute-start | bytes 6152 | tf_op jit(solution)/shard_map/ppermute | solution.py:26
  137.7 5.6 %collective-permute-start.10 = (s32[512]{0:T(512)S(1)}, s32[512]{0:T(512)S(1)}, u32[]{:S(2)}, u32[]{:S(2)}) collective-permute-start(s32[512]{0:T(512)S(1)} %collective-permute-done.9), channel_id=1, source_target_pairs={{8,0},{16,8},{24,16},{32,24},{40,32},{48,40},{56,48},{64,56},{72,6... | collective-permute-start | bytes 6152 | tf_op jit(solution)/shard_map/ppermute | solution.py:26
  144.6 5.6 %collective-permute-start.11 = (s32[512]{0:T(512)S(1)}, s32[512]{0:T(512)S(1)}, u32[]{:S(2)}, u32[]{:S(2)}) collective-permute-start(s32[512]{0:T(512)S(1)} %collective-permute-done.10), channel_id=1, source_target_pairs={{8,0},{16,8},{24,16},{32,24},{40,32},{48,40},{56,48},{64,56},{72,6... | collective-permute-start | bytes 6152 | tf_op jit(solution)/shard_map/ppermute | solution.py:26
  151.5 5.6 %collective-permute-start.12 = (s32[512]{0:T(512)S(1)}, s32[512]{0:T(512)S(1)}, u32[]{:S(2)}, u32[]{:S(2)}) collective-permute-start(s32[512]{0:T(512)S(1)} %collective-permute-done.11), channel_id=1, source_target_pairs={{8,0},{16,8},{24,16},{32,24},{40,32},{48,40},{56,48},{64,56},{72,6... | collective-permute-start | bytes 6152 | tf_op jit(solution)/shard_map/ppermute | solution.py:26
  158.4 5.6 %collective-permute-start.13 = (s32[512]{0:T(512)S(1)}, s32[512]{0:T(512)S(1)}, u32[]{:S(2)}, u32[]{:S(2)}) collective-permute-start(s32[512]{0:T(512)S(1)} %collective-permute-done.12), channel_id=1, source_target_pairs={{8,0},{16,8},{24,16},{32,24},{40,32},{48,40},{56,48},{64,56},{72,6... | collective-permute-start | bytes 6152 | tf_op jit(solution)/shard_map/ppermute | solution.py:26
  164.3 20.9 %reduce-scatter.2.cloned.1.call-done = f32[512,768]{1,0:T(8,128)} async-done(((f32[4096,768]{1,0:T(8,128)}), f32[512,768]{1,0:T(8,128)}) %reduce-scatter.2.cloned.1.call-update) | async-done | bytes 1572880 | tf_op jit(solution)/shard_map/reduce_scatter | solution.py:101
  185.2 4.6 %scatter_custom_fusion = bf16[1024,768]{1,0:T(8,128)(2,1)} fusion(s32[512]{0:T(512)S(1)} %bitcast.142, f32[512,768]{1,0:T(8,128)} %reduce-scatter.2.cloned.1.call-done, bf16[]{:T(256)} %constant.44.clone.1), kind=kCustom, calls=%fused_computation.66 | custom fusion | flops 393216 | bytes 3145730 | tf_op jit(solution)/shard_map/scatter | solution.py:114
  189.9 7.2 %all-to-all-start = ((bf16[16,64,768]{2,1,0:T(8,128)(2,1)}), bf16[16,64,768]{2,1,0:T(8,128)(2,1)}, u32[]{:S(2)}, u32[]{:S(2)}) async-start(bf16[16,64,768]{2,1,0:T(8,128)(2,1)} %bitcast.130), calls=%async_computation.1 | async-start | bytes 3145728 | tf_op jit(solution)/shard_map/all_to_all | solution.py:116
  197.2 5.3 %collective-permute-start.14 = (s32[512]{0:T(512)S(1)}, s32[512]{0:T(512)S(1)}, u32[]{:S(2)}, u32[]{:S(2)}) collective-permute-start(s32[512]{0:T(512)S(1)} %collective-permute-done.13), channel_id=1, source_target_pairs={{8,0},{16,8},{24,16},{32,24},{40,32},{48,40},{56,48},{64,56},{72,6... | collective-permute-start | bytes 6152 | tf_op jit(solution)/shard_map/ppermute | solution.py:26
  202.6 19.2 %collective-permute-done.14 = s32[512]{0:T(512)S(1)} collective-permute-done((s32[512]{0:T(512)S(1)}, s32[512]{0:T(512)S(1)}, u32[]{:S(2)}, u32[]{:S(2)}) %collective-permute-start.14) | collective-permute-done | bytes 2080 | tf_op jit(solution)/shard_map/ppermute | solution.py:26
  227.1 2.3 slice.54
  229.3 3.1 fusion.57
  232.5 2.3 copy.21
  237.7 2.4 copy.19
  241.3 73.7 %while.11 = (s32[]{:T(128)}, bf16[8,128,4,128]{3,2,1,0:T(4,128)(2,1)}, bf16[8,128,4,128]{3,1,2,0:T(8,128)(2,1)}, bf16[4096,128]{1,0:T(8,128)(2,1)}, s32[1024]{0:...) while((s32[]{:T(128)}, ...), condition=%wide.region_15.17_spmd.clone, body=%wide.region_10.16_spmd.clone.sunk | while | flops 1365182464 | bytes 41082088 | solution.py:161
  243.2 2.3 multiply_reduce_fusion.2
  252.4 2.3 multiply_reduce_fusion.2
  261.7 2.3 multiply_reduce_fusion.2
  270.9 2.3 multiply_reduce_fusion.2
  289.3 2.3 multiply_reduce_fusion.2
  298.5 2.3 multiply_reduce_fusion.2
  307.7 2.3 multiply_reduce_fusion.2
  315.0 2.3 reshape.328
  317.3 6.5 %all-to-all-start.1 = ((bf16[16,64,512]{2,1,0:T(8,128)(2,1)}), bf16[16,64,512]{2,1,0:T(8,128)(2,1)S(1)}, u32[]{:S(2)}, u32[]{:S(2)}) async-start(bf16[16,64,512]{2,1,0:T(8,128)(2,1)} %reshape.328), calls=%async_computation.2 | async-start | bytes 2097152 | tf_op jit(solution)/shard_map/all_to_all | solution.py:168
  323.8 17.8 %all-to-all-done.1 = bf16[16,64,512]{2,1,0:T(8,128)(2,1)S(1)} async-done(((bf16[16,64,512]{2,1,0:T(8,128)(2,1)}), bf16[16,64,512]{2,1,0:T(8,128)(2,1)S(1)}, u32[]{:S(2)}, u32[]{:S(2)}) %all-to-all-start.1) | async-done | bytes 1048608 | tf_op jit(solution)/shard_map/all_to_all | solution.py:168
  341.6 2.6 gather_fusion.1
  (218 shorter events, 83.4 us)
Async XLA Ops:
  6.5 114.9 %copy-start = (bf16[64,128,1,128]{3,1,2,0:T(8,128)(2,1)S(1)}, bf16[64,128,1,128]{3,1,2,0:T(8,128)(2,1)}, u32[]{:S(2)}) copy-start(bf16[64,128,1,128]{3,1,2,0:T(8,128)(2,1)} %param.19) | copy-start | bytes 6291460
  6.5 4.3 %copy-start.4 = (bf16[1024]{0:T(1024)(128)(2,1)S(1)}, bf16[1024]{0:T(1024)(128)(2,1)}, u32[]{:S(2)}) copy-start(bf16[1024]{0:T(1024)(128)(2,1)} %param.14) | copy-start | bytes 6148
  6.5 96.0 %all-gather.2.cloned.1.call-start = ((), (), s32[]{:S(2)}) async-start(), calls=%async_computation.3 | async-start | bytes 13369344 | tf_op jit(solution)/shard_map/all_gather | solution.py:98
  10.7 174.5 %reduce-scatter.2.cloned.1.call-start = ((), (), s32[]{:S(2)}) async-start(), calls=%async_computation.4 | async-start | bytes 14155776 | tf_op jit(solution)/shard_map/reduce_scatter | solution.py:101
  115.4 6.0 %copy-start.5 = (s32[1,32]{1,0:T(1,128)S(1)}, s32[1,32]{1,0:T(1,128)}, u32[]{:S(2)}) copy-start(s32[1,32]{1,0:T(1,128)} %param.21) | copy-start | bytes 388
  116.1 13.7 %collective-permute-start = (s32[512]{0:T(512)S(1)}, s32[512]{0:T(512)S(1)}, u32[]{:S(2)}, u32[]{:S(2)}) collective-permute-start(s32[512]{0:T(512)S(1)} %bitcast.137), channel_id=1, source_target_pairs={{0,8},{8,16},{16,24},{24,32},{32,40},{40,48},{48,56},{56,64},{64,7... | collective-permute-start | bytes 6152 | tf_op jit(solution)/shard_map/ppermute | solution.py:24
  117.6 13.4 %collective-permute-start.8 = (s32[512]{0:T(512)S(1)}, s32[512]{0:T(512)S(1)}, u32[]{:S(2)}, u32[]{:S(2)}) collective-permute-start(s32[512]{0:T(512)S(1)} %bitcast.138), channel_id=1, source_target_pairs={{8,0},{16,8},{24,16},{32,24},{40,32},{48,40},{56,48},{64,56},{72,6... | collective-permute-start | bytes 6152 | tf_op jit(solution)/shard_map/ppermute | solution.py:26
  129.8 6.9 %collective-permute-start.1 = (s32[512]{0:T(512)S(1)}, s32[512]{0:T(512)S(1)}, u32[]{:S(2)}, u32[]{:S(2)}) collective-permute-start(s32[512]{0:T(512)S(1)} %collective-permute-done), channel_id=1, source_target_pairs={{0,8},{8,16},{16,24},{24,32},{32,40},{40,48},{48,56},{56,64},{64,7... | collective-permute-start | bytes 6152 | tf_op jit(solution)/shard_map/ppermute | solution.py:24
  131.0 6.7 %collective-permute-start.9 = (s32[512]{0:T(512)S(1)}, s32[512]{0:T(512)S(1)}, u32[]{:S(2)}, u32[]{:S(2)}) collective-permute-start(s32[512]{0:T(512)S(1)} %collective-permute-done.8), channel_id=1, source_target_pairs={{8,0},{16,8},{24,16},{32,24},{40,32},{48,40},{56,48},{64,56},{72,6... | collective-permute-start | bytes 6152 | tf_op jit(solution)/shard_map/ppermute | solution.py:26
  136.7 6.9 %collective-permute-start.2 = (s32[512]{0:T(512)S(1)}, s32[512]{0:T(512)S(1)}, u32[]{:S(2)}, u32[]{:S(2)}) collective-permute-start(s32[512]{0:T(512)S(1)} %collective-permute-done.1), channel_id=1, source_target_pairs={{0,8},{8,16},{16,24},{24,32},{32,40},{40,48},{48,56},{56,64},{64,7... | collective-permute-start | bytes 6152 | tf_op jit(solution)/shard_map/ppermute | solution.py:24
  137.7 6.9 %collective-permute-start.10 = (s32[512]{0:T(512)S(1)}, s32[512]{0:T(512)S(1)}, u32[]{:S(2)}, u32[]{:S(2)}) collective-permute-start(s32[512]{0:T(512)S(1)} %collective-permute-done.9), channel_id=1, source_target_pairs={{8,0},{16,8},{24,16},{32,24},{40,32},{48,40},{56,48},{64,56},{72,6... | collective-permute-start | bytes 6152 | tf_op jit(solution)/shard_map/ppermute | solution.py:26
  143.6 6.9 %collective-permute-start.3 = (s32[512]{0:T(512)S(1)}, s32[512]{0:T(512)S(1)}, u32[]{:S(2)}, u32[]{:S(2)}) collective-permute-start(s32[512]{0:T(512)S(1)} %collective-permute-done.2), channel_id=1, source_target_pairs={{0,8},{8,16},{16,24},{24,32},{32,40},{40,48},{48,56},{56,64},{64,7... | collective-permute-start | bytes 6152 | tf_op jit(solution)/shard_map/ppermute | solution.py:24
  144.6 6.9 %collective-permute-start.11 = (s32[512]{0:T(512)S(1)}, s32[512]{0:T(512)S(1)}, u32[]{:S(2)}, u32[]{:S(2)}) collective-permute-start(s32[512]{0:T(512)S(1)} %collective-permute-done.10), channel_id=1, source_target_pairs={{8,0},{16,8},{24,16},{32,24},{40,32},{48,40},{56,48},{64,56},{72,6... | collective-permute-start | bytes 6152 | tf_op jit(solution)/shard_map/ppermute | solution.py:26
  150.5 6.9 %collective-permute-start.4 = (s32[512]{0:T(512)S(1)}, s32[512]{0:T(512)S(1)}, u32[]{:S(2)}, u32[]{:S(2)}) collective-permute-start(s32[512]{0:T(512)S(1)} %collective-permute-done.3), channel_id=1, source_target_pairs={{0,8},{8,16},{16,24},{24,32},{32,40},{40,48},{48,56},{56,64},{64,7... | collective-permute-start | bytes 6152 | tf_op jit(solution)/shard_map/ppermute | solution.py:24
  151.5 6.9 %collective-permute-start.12 = (s32[512]{0:T(512)S(1)}, s32[512]{0:T(512)S(1)}, u32[]{:S(2)}, u32[]{:S(2)}) collective-permute-start(s32[512]{0:T(512)S(1)} %collective-permute-done.11), channel_id=1, source_target_pairs={{8,0},{16,8},{24,16},{32,24},{40,32},{48,40},{56,48},{64,56},{72,6... | collective-permute-start | bytes 6152 | tf_op jit(solution)/shard_map/ppermute | solution.py:26
  157.4 6.9 %collective-permute-start.5 = (s32[512]{0:T(512)S(1)}, s32[512]{0:T(512)S(1)}, u32[]{:S(2)}, u32[]{:S(2)}) collective-permute-start(s32[512]{0:T(512)S(1)} %collective-permute-done.4), channel_id=1, source_target_pairs={{0,8},{8,16},{16,24},{24,32},{32,40},{40,48},{48,56},{56,64},{64,7... | collective-permute-start | bytes 6152 | tf_op jit(solution)/shard_map/ppermute | solution.py:24
  158.4 38.8 %collective-permute-start.13 = (s32[512]{0:T(512)S(1)}, s32[512]{0:T(512)S(1)}, u32[]{:S(2)}, u32[]{:S(2)}) collective-permute-start(s32[512]{0:T(512)S(1)} %collective-permute-done.12), channel_id=1, source_target_pairs={{8,0},{16,8},{24,16},{32,24},{40,32},{48,40},{56,48},{64,56},{72,6... | collective-permute-start | bytes 6152 | tf_op jit(solution)/shard_map/ppermute | solution.py:26
  164.3 38.1 %collective-permute-start.6 = (s32[512]{0:T(512)S(1)}, s32[512]{0:T(512)S(1)}, u32[]{:S(2)}, u32[]{:S(2)}) collective-permute-start(s32[512]{0:T(512)S(1)} %collective-permute-done.5), channel_id=1, source_target_pairs={{0,8},{8,16},{16,24},{24,32},{32,40},{40,48},{48,56},{56,64},{64,7... | collective-permute-start | bytes 6152 | tf_op jit(solution)/shard_map/ppermute | solution.py:24
  189.9 35.4 %all-to-all-start = ((bf16[16,64,768]{2,1,0:T(8,128)(2,1)}), bf16[16,64,768]{2,1,0:T(8,128)(2,1)}, u32[]{:S(2)}, u32[]{:S(2)}) async-start(bf16[16,64,768]{2,1,0:T(8,128)(2,1)} %bitcast.130), calls=%async_computation.1 | async-start | bytes 3145728 | tf_op jit(solution)/shard_map/all_to_all | solution.py:116
  197.2 24.6 %collective-permute-start.14 = (s32[512]{0:T(512)S(1)}, s32[512]{0:T(512)S(1)}, u32[]{:S(2)}, u32[]{:S(2)}) collective-permute-start(s32[512]{0:T(512)S(1)} %collective-permute-done.13), channel_id=1, source_target_pairs={{8,0},{16,8},{24,16},{32,24},{40,32},{48,40},{56,48},{64,56},{72,6... | collective-permute-start | bytes 6152 | tf_op jit(solution)/shard_map/ppermute | solution.py:26
  202.4 19.3 %collective-permute-start.7 = (s32[512]{0:T(512)S(1)}, s32[512]{0:T(512)S(1)}, u32[]{:S(2)}, u32[]{:S(2)}) collective-permute-start(s32[512]{0:T(512)S(1)} %collective-permute-done.6), channel_id=1, source_target_pairs={{0,8},{8,16},{16,24},{24,32},{32,40},{40,48},{48,56},{56,64},{64,7... | collective-permute-start | bytes 6152 | tf_op jit(solution)/shard_map/ppermute | solution.py:24
  241.5 1.7 copy-start.1
  250.7 1.7 copy-start.1
  259.9 1.7 copy-start.1
  266.0 1.5 copy-start.2
  269.1 1.7 copy-start.1
  275.2 1.5 copy-start.2
  278.3 1.7 copy-start.1
  287.5 1.7 copy-start.1
  296.7 1.7 copy-start.1
  305.9 1.7 copy-start.1
  317.3 24.3 %all-to-all-start.1 = ((bf16[16,64,512]{2,1,0:T(8,128)(2,1)}), bf16[16,64,512]{2,1,0:T(8,128)(2,1)S(1)}, u32[]{:S(2)}, u32[]{:S(2)}) async-start(bf16[16,64,512]{2,1,0:T(8,128)(2,1)} %reshape.328), calls=%async_computation.2 | async-start | bytes 2097152 | tf_op jit(solution)/shard_map/all_to_all | solution.py:168
  (7 other events, 9.7 us)
Sparse Core Ops, SparseCore 0:
  10.9 91.6 all-gather.1
  115.5 69.6 reduce-scatter.1
